TPU v7x, 128 devices: a whole 4x4x4 slice. The times are simulated.
128 devices in a mesh: dp: 128 (over x, y, z, core).
Axes of the slice: x: 4, y: 4, z: 4, core: 2. Of those that a mesh axis runs over, the one named last changes fastest.
Arguments:
- hidden_in: bfloat16 [32768, 4096], P('dp'), may hold values from -24 to 24
- queries: bfloat16 [32768, 2048], P('dp'), may hold values from -16 to 16
- keys: bfloat16 [32768, 512], P('dp'), may hold values from -16 to 16
- values: bfloat16 [32768, 512], P('dp'), may hold values from -6 to 6
- grad_attn: bfloat16 [32768, 2048], P('dp'), may hold values from -6 to 6
- send_rows: int32 [4, 128], replicated, may hold values from -1 to 255, as said below
- slot_docs: int32 [128, 4], P('dp'), may hold values from -1 to 255, as said below
Outputs:
- grad_queries: bfloat16 [32768, 2048], P('dp')
- grad_keys: bfloat16 [32768, 512], P('dp')
- grad_values: bfloat16 [32768, 512], P('dp')
- grad_wv: float32 [4096, 512], P('dp')
Inputs may be any that keep to these rules, and one draw needn't show every extreme that they name: `send_rows`: every owner sends the same local rows to a rank. Each local row appears exactly once. The rows sent to one rank form whole documents at consecutive slots, the local rows of a document consecutive and rising with the slot; a document has at most 4 local rows, and in every draw some rank has all 4 slots used. slot_docs[r, j] is -1 exactly where send_rows[j, r] is -1; slots with the same number hold one document, and distinct documents have distinct numbers.
All inputs are finite; a program needn't handle non-finite values.
Results may differ from a plain program's by a relative error of at most 0.0057.
Values may be sent and summed in bfloat16 or wider, within the bound.
No kernel may reach another device: no remote copies, remote signals or barrier semaphores. Data moves between devices by JAX's collectives and lax.ppermute only.
A program may use at most 128 MiB of HBM per device.

v0:
```python
import math

import jax
import jax.numpy as jnp
from jax import lax
from jax.sharding import PartitionSpec as P

HQ = 16
HK = 4
DH = 128


def attend_rows(q_rows, k_rows, v_rows, o_rows, segment):
    row_count = q_rows.shape[0]
    group_size = HQ // HK
    score_scale = 1.0 / math.sqrt(DH)
    order_ids = jnp.arange(row_count, dtype=jnp.int32)
    live_rows = segment >= 0
    allowed = (
        (segment[:, None] == segment[None, :])
        & (order_ids[None, :] <= order_ids[:, None])
        & live_rows[:, None]
    )
    q_four = q_rows.reshape(row_count, HK, group_size, DH)
    o_four = o_rows.reshape(row_count, HK, group_size, DH)
    k_three = k_rows.reshape(row_count, HK, DH)
    v_three = v_rows.reshape(row_count, HK, DH)
    grad_q_list = []
    grad_k_list = []
    grad_v_list = []
    for head_kv in range(HK):
        q_group = q_four[:, head_kv]
        o_group = o_four[:, head_kv]
        k_group = k_three[:, head_kv]
        v_group = v_three[:, head_kv]
        scores = (
            jnp.einsum("qhd,kd->hqk", q_group, k_group, preferred_element_type=jnp.float32)
            * score_scale
        )
        scores = jnp.where(allowed[None], scores, jnp.float32(-1000000000.0))
        row_max = jnp.max(scores, axis=-1, keepdims=True)
        weights = jnp.exp(scores - row_max)
        attn_probs = weights / jnp.sum(weights, axis=-1, keepdims=True)
        attn_probs = jnp.where(live_rows[None, :, None], attn_probs, jnp.float32(0.0))
        probs_b = attn_probs.astype(jnp.bfloat16)
        grad_v_list.append(
            jnp.einsum("hqk,qhd->kd", probs_b, o_group, preferred_element_type=jnp.float32)
        )
        dprob = jnp.einsum("qhd,kd->hqk", o_group, v_group, preferred_element_type=jnp.float32)
        row_delta = jnp.sum(attn_probs * dprob, axis=-1, keepdims=True)
        dscore = (attn_probs * (dprob - row_delta) * score_scale).astype(jnp.bfloat16)
        grad_q_list.append(
            jnp.einsum("hqk,kd->qhd", dscore, k_group, preferred_element_type=jnp.float32)
        )
        grad_k_list.append(
            jnp.einsum("hqk,qhd->kd", dscore, q_group, preferred_element_type=jnp.float32)
        )
    grad_q_rows = jnp.stack(grad_q_list, axis=1).reshape(row_count, HQ * DH).astype(jnp.bfloat16)
    grad_k_rows = jnp.stack(grad_k_list, axis=1).reshape(row_count, HK * DH).astype(jnp.bfloat16)
    grad_v_rows = jnp.stack(grad_v_list, axis=1).reshape(row_count, HK * DH).astype(jnp.bfloat16)
    return (grad_q_rows, grad_k_rows, grad_v_rows)


def local(hidden_in, queries, keys, values, grad_attn, send_rows, slot_docs):
    owners = lax.axis_size("dp")
    slot_count = send_rows.shape[0]
    tok_rows = queries.shape[0]
    live_send = send_rows >= 0
    pick_rows = jnp.maximum(send_rows, 0)
    grad_scale = 1.0 / math.sqrt(tok_rows * owners)

    def pack_rows(table):
        return jnp.where(live_send[:, :, None], table[pick_rows], jnp.zeros((), table.dtype))

    def flatten(block):
        return block.reshape(slot_count * owners, block.shape[2])

    def unflatten(block):
        return block.reshape(slot_count, owners, block.shape[1])

    targets = jnp.where(live_send, send_rows, tok_rows).reshape(-1)

    def place_rows(block):
        return (
            jnp.zeros((tok_rows, block.shape[2]), block.dtype)
            .at[targets]
            .set(flatten(block), mode="drop")
        )

    widths = (queries.shape[1], keys.shape[1], values.shape[1], grad_attn.shape[1])
    bounds = [sum(widths[:i]) for i in range(len(widths) + 1)]
    table = jnp.concatenate((queries, keys, values, grad_attn), axis=1)
    rows_in = flatten(
        lax.all_to_all(pack_rows(table), "dp", split_axis=1, concat_axis=1, tiled=True)
    )
    q_in, k_in, v_in, o_in = (rows_in[:, bounds[i] : bounds[i + 1]] for i in range(len(widths)))
    segment = jnp.broadcast_to(slot_docs[0][:, None], (slot_count, owners)).reshape(-1)
    grad_q_rows, grad_k_rows, grad_v_rows = attend_rows(q_in, k_in, v_in, o_in, segment)
    rows_out = jnp.concatenate((grad_q_rows, grad_k_rows, grad_v_rows), axis=1)
    home = place_rows(
        lax.all_to_all(unflatten(rows_out), "dp", split_axis=1, concat_axis=1, tiled=True)
    )
    grad_queries = home[:, bounds[0] : bounds[1]]
    grad_keys = home[:, bounds[1] : bounds[2]]
    grad_values = home[:, bounds[2] : bounds[3]]
    partial = jnp.einsum("td,tc->dc", hidden_in, grad_values, preferred_element_type=jnp.float32)
    partial = partial.reshape(owners, partial.shape[0] // owners, partial.shape[1])
    grad_wv = lax.all_to_all(partial, "dp", 0, 0, tiled=True).sum(0) * grad_scale
    return (grad_queries, grad_keys, grad_values, grad_wv)


def solution(mesh):
    placed = (
        P("dp", None),
        P("dp", None),
        P("dp", None),
        P("dp", None),
        P("dp", None),
        P(),
        P("dp", None),
    )
    return jax.shard_map(
        local,
        mesh=mesh,
        in_specs=placed,
        out_specs=(P("dp", None), P("dp", None), P("dp", None), P("dp", None)),
        check_vma=False,
    )
```

profile of v0, /device:TPU:103, one launch (start us, length us, event | category | flops | bytes accessed | tf_op | source)
XLA Modules:
  0.0 443.1 jit_solution(2129745018264398708)
XLA Ops:
  0.6 0.8 broadcast_compare_fusion
  1.5 0.7 maximum_bitcast_fusion
  2.2 0.1 copy.151
  2.3 2.9 pad_maximum_fusion.1
  5.2 12.6 %gather_fusion = bf16[512,5120]{1,0:T(8,128)(2,1)} fusion(bf16[256,5120]{1,0:T(8,128)(2,1)} %pad_maximum_fusion.1, s32[1024]{0:T(1024)S(1)} %pad_clamp_fusion), kind=kCustom, calls=%fused_computation | custom fusion | bytes 10487808 | tf_op jit(solution)/shard_map/gather | solution.py:73
  17.8 9.3 %copy_select_fusion = bf16[4,128,5120]{2,0,1:T(4,128)(2,1)} fusion(bf16[4,128,5120]{2,1,0:T(8,128)(2,1)} %bitcast.419, pred[4,128]{0,1:T(8,128)(4,1)S(1)} %copy.151), kind=kLoop, calls=%fused_computation.12 | loop fusion | flops 2621440 | bytes 10486272 | tf_op jit(solution)/shard_map/jit(_where)/select_n | solution.py:73
  27.1 11.2 %all-to-all-start = ((bf16[4,128,5120]{2,0,1:T(4,128)(2,1)}), bf16[4,128,5120]{2,0,1:T(4,128)(2,1)}, u32[]{:S(2)}, u32[]{:S(2)}) async-start(bf16[4,128,5120]{2,0,1:T(4,128)(2,1)} %copy_select_fusion), calls=%async_computation | async-start | bytes 10485760 | tf_op jit(solution)/shard_map/all_to_all | solution.py:94
  38.3 0.1 bitcast_compare_fusion
  38.4 0.2 fusion.113
  38.7 62.0 %all-to-all-done = bf16[4,128,5120]{2,0,1:T(4,128)(2,1)} async-done(((bf16[4,128,5120]{2,0,1:T(4,128)(2,1)}), bf16[4,128,5120]{2,0,1:T(4,128)(2,1)}, u32[]{:S(2)}, u32[]{:S(2)}) %all-to-all-start) | async-done | bytes 5242912 | tf_op jit(solution)/shard_map/all_to_all | solution.py:94
  100.7 11.7 %copy.153 = bf16[4,128,5120]{1,0,2:T(4,128)(2,1)} copy(bf16[4,128,5120]{2,0,1:T(4,128)(2,1)} %all-to-all-done) | data formatting | bytes 10485760 | tf_op jit(solution)/shard_map/all_to_all | solution.py:94
  112.4 3.4 copy.216
  115.8 0.3 fusion.149
  116.1 3.1 fusion.121
  119.3 2.7 fusion.119
  122.0 2.7 fusion.117
  124.6 2.7 fusion.123
  127.3 0.7 fusion.122
  128.1 2.1 fusion.151
  130.2 1.9 copy-done.11
  132.1 0.7 fusion.109
  132.8 8.7 %fusion.96 = bf16[512,1,128]{2,0,1:T(8,128)(2,1)} fusion(f32[512,512,4]{1,0,2:T(8,128)} %fusion.123, bf16[512,4,4,128]{0,3,2,1:T(8,128)(2,1)} %bitcast.424, f32[4,512,512]{1,2,0:T(8,128)} %copy-done.11, f32[4,512]{1,0:T(4,128)S(1)} %get-tuple-element.12, pred[512]{0:T(512)(128)(4,1)S(1)} %bitcast_compare_fusion), kind=kOutput, calls=%fused_computation.108 | convolution fusion | flops 277940736 | bytes 17449984 | tf_op jit(solution)/shard_map/hqk,qhd->kd/dot_general | solution.py:56
  141.5 7.9 %fusion.63 = bf16[512,1,4,128]{0,3,2,1:T(8,128)(2,1)S(1)} fusion(f32[512,512,4]{1,0,2:T(8,128)} %fusion.123, bf16[512,4,128]{0,2,1:T(8,128)(2,1)S(1)} %bitcast.441, f32[4,512,512]{1,2,0:T(8,128)} %copy-done.11, f32[4,512]{1,0:T(4,128)S(1)} %get-tuple-element.12, pred[512]{0:T(512)(128)(4,1)S(1)} %bitcast_compare_fusion), kind=kOutput, calls=%fused_computation.91 | convolution fusion | flops 278137344 | bytes 17449984 | tf_op jit(solution)/shard_map/hqk,kd->qhd/dot_general | solution.py:53
  149.4 1.8 fusion.120
  151.2 2.3 fusion.152
  153.5 1.9 copy-done.12
  155.5 2.4 fusion.106
  157.9 8.5 %fusion.97 = bf16[512,1,128]{2,0,1:T(8,128)(2,1)} fusion(f32[512,512,4]{1,0,2:T(8,128)} %fusion.121, bf16[512,4,4,128]{0,3,2,1:T(8,128)(2,1)} %bitcast.426, f32[4,512,512]{1,2,0:T(8,128)} %copy-done.12, f32[4,512]{1,0:T(4,128)S(1)} %get-tuple-element.14, pred[512]{0:T(512)(128)(4,1)S(1)} %bitcast_compare_fusion), kind=kOutput, calls=%fused_computation.109 | convolution fusion | flops 277940736 | bytes 17449984 | tf_op jit(solution)/shard_map/hqk,qhd->kd/dot_general | solution.py:56
  166.4 8.7 %fusion.62 = bf16[512,1,4,128]{0,3,2,1:T(8,128)(2,1)} fusion(f32[512,512,4]{1,0,2:T(8,128)} %fusion.121, bf16[512,4,128]{0,2,1:T(8,128)(2,1)S(1)} %bitcast.443, f32[4,512,512]{1,2,0:T(8,128)} %copy-done.12, f32[4,512]{1,0:T(4,128)S(1)} %get-tuple-element.14, pred[512]{0:T(512)(128)(4,1)S(1)} %bitcast_compare_fusion), kind=kOutput, calls=%fused_computation.90 | convolution fusion | flops 278137344 | bytes 17449984 | tf_op jit(solution)/shard_map/hqk,kd->qhd/dot_general | solution.py:53
  175.1 1.8 fusion.118
  176.9 2.1 fusion.153
  179.0 2.0 copy-done.13
  181.0 2.4 fusion.103
  183.4 8.8 %fusion.98 = bf16[512,1,128]{2,0,1:T(8,128)(2,1)} fusion(f32[512,512,4]{1,0,2:T(8,128)} %fusion.119, bf16[512,4,4,128]{0,3,2,1:T(8,128)(2,1)} %bitcast.428, f32[4,512,512]{1,2,0:T(8,128)} %copy-done.13, f32[4,512]{1,0:T(4,128)S(1)} %get-tuple-element.16, pred[512]{0:T(512)(128)(4,1)S(1)} %bitcast_compare_fusion), kind=kOutput, calls=%fused_computation.110 | convolution fusion | flops 277940736 | bytes 17449984 | tf_op jit(solution)/shard_map/hqk,qhd->kd/dot_general | solution.py:56
  192.2 8.8 %fusion.61 = bf16[512,1,4,128]{0,3,2,1:T(8,128)(2,1)} fusion(f32[512,512,4]{1,0,2:T(8,128)} %fusion.119, bf16[512,4,128]{0,2,1:T(8,128)(2,1)S(1)} %bitcast.445, f32[4,512,512]{1,2,0:T(8,128)} %copy-done.13, f32[4,512]{1,0:T(4,128)S(1)} %get-tuple-element.16, pred[512]{0:T(512)(128)(4,1)S(1)} %bitcast_compare_fusion), kind=kOutput, calls=%fused_computation.89 | convolution fusion | flops 278137344 | bytes 17449984 | tf_op jit(solution)/shard_map/hqk,kd->qhd/dot_general | solution.py:53
  201.1 1.8 fusion.116
  202.8 2.3 fusion.154
  205.2 2.0 copy-done.10
  207.1 2.4 fusion.100
  209.6 8.5 %fusion.99 = bf16[512,1,128]{2,0,1:T(8,128)(2,1)} fusion(f32[512,512,4]{1,0,2:T(8,128)} %fusion.117, bf16[512,4,4,128]{0,3,2,1:T(8,128)(2,1)} %bitcast.430, f32[4,512,512]{1,2,0:T(8,128)} %copy-done.10, f32[4,512]{1,0:T(4,128)S(1)} %get-tuple-element.18, pred[512]{0:T(512)(128)(4,1)S(1)} %bitcast_compare_fusion), kind=kOutput, calls=%fused_computation.111 | convolution fusion | flops 277940736 | bytes 17449984 | tf_op jit(solution)/shard_map/hqk,qhd->kd/dot_general | solution.py:56
  218.1 8.7 %fusion.60 = bf16[512,1,4,128]{0,3,2,1:T(8,128)(2,1)} fusion(f32[512,512,4]{1,0,2:T(8,128)} %fusion.117, bf16[512,4,128]{0,2,1:T(8,128)(2,1)S(1)} %bitcast.447, f32[4,512,512]{1,2,0:T(8,128)} %copy-done.10, f32[4,512]{1,0:T(4,128)S(1)} %get-tuple-element.18, pred[512]{0:T(512)(128)(4,1)S(1)} %bitcast_compare_fusion), kind=kOutput, calls=%fused_computation.88 | convolution fusion | flops 278137344 | bytes 17449984 | tf_op jit(solution)/shard_map/hqk,kd->qhd/dot_general | solution.py:53
  226.8 3.0 pad_maximum_fusion.2
  229.8 4.0 convert_element_type.43
  233.9 5.6 %copy.180 = bf16[4,128,2048]{2,0,1:T(4,128)(2,1)} copy(bf16[4,128,2048]{1,0,2:T(4,128)(2,1)} %convert_element_type.43) | data formatting | bytes 4194304 | tf_op jit(solution)/shard_map/convert_element_type | solution.py:58
  239.5 0.4 copy.178
  240.0 0.2 convert_element_type.44
  240.2 0.4 copy.181
  240.6 1.0 pad_maximum_fusion.4
  241.6 0.4 copy.179
  242.0 1.0 convert_element_type.49
  243.0 1.4 copy.182
  244.5 4.8 %pad_maximum_fusion = bf16[4,128,3072]{2,0,1:T(4,128)(2,1)} fusion(bf16[4,128,512]{2,0,1:T(4,128)(2,1)S(1)} %copy.182, bf16[4,128,512]{2,0,1:T(4,128)(2,1)S(1)} %copy.181, bf16[4,128,2048]{2,0,1:T(4,128)(2,1)} %copy.180), kind=kLoop, calls=%fused_computation.49 | loop fusion | flops 9437184 | bytes 6291456 | tf_op jit(solution)/shard_map/concatenate | solution.py:99
  249.3 9.8 %all-to-all-start.1 = ((bf16[4,128,3072]{2,0,1:T(4,128)(2,1)}), bf16[4,128,3072]{2,0,1:T(4,128)(2,1)}, u32[]{:S(2)}, u32[]{:S(2)}) async-start(bf16[4,128,3072]{2,0,1:T(4,128)(2,1)} %pad_maximum_fusion), calls=%async_computation.1 | async-start | bytes 6291456 | tf_op jit(solution)/shard_map/all_to_all | solution.py:101
  259.0 36.7 %all-to-all-done.1 = bf16[4,128,3072]{2,0,1:T(4,128)(2,1)} async-done(((bf16[4,128,3072]{2,0,1:T(4,128)(2,1)}), bf16[4,128,3072]{2,0,1:T(4,128)(2,1)}, u32[]{:S(2)}, u32[]{:S(2)}) %all-to-all-start.1) | async-done | bytes 3145760 | tf_op jit(solution)/shard_map/all_to_all | solution.py:101
  295.8 4.5 %copy.183 = bf16[4,128,3072]{2,1,0:T(8,128)(2,1)} copy(bf16[4,128,3072]{2,0,1:T(4,128)(2,1)} %all-to-all-done.1) | data formatting | bytes 6291456 | tf_op jit(solution)/shard_map/all_to_all | solution.py:101
  300.3 7.3 %scatter_custom_fusion = bf16[256,3072]{1,0:T(8,128)(2,1)} fusion(s32[512]{0:T(512)S(1)} %bitcast.453, bf16[512,3072]{1,0:T(8,128)(2,1)} %bitcast.439, bf16[]{:T(256)} %constant.8.clone.1), kind=kCustom, calls=%fused_computation.119 | custom fusion | bytes 1573376 | tf_op jit(solution)/shard_map/scatter | solution.py:87
  307.6 1.8 fusion.150
  309.4 4.5 %convolution_bitcast_fusion = f32[4096,512]{0,1:T(8,128)} fusion(bf16[256,512]{1,0:T(8,128)(2,1)S(1)} %get-tuple-element.8, bf16[256,4096]{1,0:T(8,128)(2,1)S(1)} %copy-done), kind=kOutput, calls=%fused_computation.10 | convolution fusion | flops 1073741824 | bytes 10747904 | tf_op jit(solution)/shard_map/td,tc->dc/dot_general | solution.py:106
  313.9 9.0 %copy.184 = f32[4096,512]{1,0:T(8,128)} copy(f32[4096,512]{0,1:T(8,128)} %convolution_bitcast_fusion) | data formatting | bytes 16777216 | tf_op jit(solution)/shard_map/td,tc->dc/dot_general | solution.py:106
  322.9 10.5 %all-to-all-start.2 = ((f32[128,32,512]{2,1,0:T(8,128)}), f32[128,32,512]{2,1,0:T(8,128)}, u32[]{:S(2)}, u32[]{:S(2)}) async-start(f32[128,32,512]{2,1,0:T(8,128)} %bitcast.418), calls=%async_computation.2 | async-start | bytes 16777216 | tf_op jit(solution)/shard_map/all_to_all | solution.py:108
  333.4 2.3 slice.114
  335.7 102.4 %all-to-all-done.2 = f32[128,32,512]{2,1,0:T(8,128)} async-done(((f32[128,32,512]{2,1,0:T(8,128)}), f32[128,32,512]{2,1,0:T(8,128)}, u32[]{:S(2)}, u32[]{:S(2)}) %all-to-all-start.2) | async-done | bytes 8388640 | tf_op jit(solution)/shard_map/all_to_all | solution.py:108
  438.1 3.9 reduce_sum.89
  442.1 0.6 broadcast_multiply_fusion
  (29 shorter events, 0.3 us)
Async XLA Ops:
  0.6 308.8 %copy-start = (bf16[256,4096]{1,0:T(8,128)(2,1)S(1)}, bf16[256,4096]{1,0:T(8,128)(2,1)}, u32[]{:S(2)}) copy-start(bf16[256,4096]{1,0:T(8,128)(2,1)} %param.7) | copy-start | bytes 6291460
  27.1 11.2 %copy-start.9 = (s32[1,4]{1,0:T(1,128)S(1)}, s32[1,4]{1,0:T(1,128)}, u32[]{:S(2)}) copy-start(s32[1,4]{1,0:T(1,128)} %param.13) | copy-start | bytes 52
  27.1 73.6 %all-to-all-start = ((bf16[4,128,5120]{2,0,1:T(4,128)(2,1)}), bf16[4,128,5120]{2,0,1:T(4,128)(2,1)}, u32[]{:S(2)}, u32[]{:S(2)}) async-start(bf16[4,128,5120]{2,0,1:T(4,128)(2,1)} %copy_select_fusion), calls=%async_computation | async-start | bytes 10485760 | tf_op jit(solution)/shard_map/all_to_all | solution.py:94
  116.1 11.2 %copy-start.1 = (bf16[512,2048]{0,1:T(8,128)(2,1)}, bf16[512,2048]{0,1:T(8,128)(2,1)S(1)}, u32[]{:S(2)}) copy-start(bf16[512,2048]{0,1:T(8,128)(2,1)S(1)} %get-tuple-element.6) | copy-start | bytes 6291460
  116.1 14.1 %copy-start.2 = (bf16[512,2048]{0,1:T(8,128)(2,1)}, bf16[512,2048]{0,1:T(8,128)(2,1)S(1)}, u32[]{:S(2)}) copy-start(bf16[512,2048]{0,1:T(8,128)(2,1)S(1)} %get-tuple-element.7) | copy-start | bytes 6291460
  130.2 1.9 copy-start.11
  153.5 2.0 copy-start.12
  179.0 2.0 copy-start.13
  205.2 2.0 copy-start.10
  229.8 9.6 %copy-start.5 = (bf16[512,1,128]{2,0,1:T(8,128)(2,1)S(1)}, bf16[512,1,128]{2,0,1:T(8,128)(2,1)}, u32[]{:S(2)}) copy-start(bf16[512,1,128]{2,0,1:T(8,128)(2,1)} %fusion.96) | copy-start | bytes 393220
  229.8 9.6 %copy-start.6 = (bf16[512,1,128]{2,0,1:T(8,128)(2,1)S(1)}, bf16[512,1,128]{2,0,1:T(8,128)(2,1)}, u32[]{:S(2)}) copy-start(bf16[512,1,128]{2,0,1:T(8,128)(2,1)} %fusion.97) | copy-start | bytes 393220
  229.8 9.6 %copy-start.7 = (bf16[512,1,128]{2,0,1:T(8,128)(2,1)S(1)}, bf16[512,1,128]{2,0,1:T(8,128)(2,1)}, u32[]{:S(2)}) copy-start(bf16[512,1,128]{2,0,1:T(8,128)(2,1)} %fusion.98) | copy-start | bytes 393220
  229.8 9.6 %copy-start.8 = (bf16[512,1,128]{2,0,1:T(8,128)(2,1)S(1)}, bf16[512,1,128]{2,0,1:T(8,128)(2,1)}, u32[]{:S(2)}) copy-start(bf16[512,1,128]{2,0,1:T(8,128)(2,1)} %fusion.99) | copy-start | bytes 393220
  233.9 6.7 %copy-start.4 = (bf16[512,1,128]{2,0,1:T(8,128)(2,1)S(1)}, bf16[512,1,128]{2,0,1:T(8,128)(2,1)}, u32[]{:S(2)}) copy-start(bf16[512,1,128]{2,0,1:T(8,128)(2,1)} %fusion.106) | copy-start | bytes 393220
  249.3 46.5 %all-to-all-start.1 = ((bf16[4,128,3072]{2,0,1:T(4,128)(2,1)}), bf16[4,128,3072]{2,0,1:T(4,128)(2,1)}, u32[]{:S(2)}, u32[]{:S(2)}) async-start(bf16[4,128,3072]{2,0,1:T(4,128)(2,1)} %pad_maximum_fusion), calls=%async_computation.1 | async-start | bytes 6291456 | tf_op jit(solution)/shard_map/all_to_all | solution.py:101
  309.4 4.5 %copy-start.3 = (bf16[256,512]{1,0:T(8,128)(2,1)}, bf16[256,512]{1,0:T(8,128)(2,1)S(1)}, u32[]{:S(2)}) copy-start(bf16[256,512]{1,0:T(8,128)(2,1)S(1)} %get-tuple-element.8) | copy-start | bytes 786436
  322.9 115.2 %all-to-all-start.2 = ((f32[128,32,512]{2,1,0:T(8,128)}), f32[128,32,512]{2,1,0:T(8,128)}, u32[]{:S(2)}, u32[]{:S(2)}) async-start(f32[128,32,512]{2,1,0:T(8,128)} %bitcast.418), calls=%async_computation.2 | async-start | bytes 16777216 | tf_op jit(solution)/shard_map/all_to_all | solution.py:108
where the time goes:
time: 452 us; the launch traced here: 443 us
  waiting for transfers between devices  201 us (44%)
  matrix products  98.4 us (22%)
  local copies, waits for them, and re-layouts  74.4 us (16%)
  other arithmetic  36.4 us (8%)
  starting transfers between devices  31.4 us (7%)
    all_to_all x1, waiting for transfers between devices, local(): lax.all_to_all(partial, 'dp', 0, 0, tiled=True).sum(0) * grad_scale  102 us
    all_to_all x1, waiting for transfers between devices, local(): lax.all_to_all(pack_rows(table), 'dp', split_axis=1, concat_axis=1, tiled...  62 us
    all_to_all x1, waiting for transfers between devices, local(): lax.all_to_all(unflatten(rows_out), 'dp', split_axis=1, concat_axis=1, ti...  36.7 us
    dot_general x4, matrix products, attend_rows(): jnp.einsum('hqk,qhd->kd', dscore, q_group, preferred_element_type=jnp.flo...  34.5 us
    dot_general x4, matrix products, attend_rows(): jnp.einsum('hqk,kd->qhd', dscore, k_group, preferred_element_type=jnp.flo...  34.1 us
    gather x1, local copies, waits for them, and re-layouts, pack_rows(): table[pick_rows]  12.6 us
    all_to_all x1, local copies, waits for them, and re-layouts, local(): lax.all_to_all(pack_rows(table), 'dp', split_axis=1, concat_axis=1, tiled...  11.7 us
    unnamed x29, local copies, waits for them, and re-layouts  11.2 us
  transfers between devices with their start and end apart: 3, of which 3 were waited for; matrix products, arithmetic and copies ran while one was open for 1% of the time, Pallas kernels for 0%

commit v1 on v0

v1 whole, which is shorter than its diff:
```python
import math

import jax
import jax.numpy as jnp
from jax import lax
from jax.sharding import PartitionSpec as P

HQ = 16
HK = 4
DH = 128


def attend_group(q_group, k_group, v_group, o_group, segment):
    row_count = q_group.shape[0]
    group_size = HQ // HK
    score_scale = 1.0 / math.sqrt(DH)
    order_ids = jnp.arange(row_count, dtype=jnp.int32)
    live_rows = segment >= 0
    allowed = (
        (segment[:, None] == segment[None, :])
        & (order_ids[None, :] <= order_ids[:, None])
        & live_rows[:, None]
    )
    q_group = q_group.reshape(row_count, group_size, DH)
    o_group = o_group.reshape(row_count, group_size, DH)
    scores = (
        jnp.einsum("qhd,kd->hqk", q_group, k_group, preferred_element_type=jnp.float32)
        * score_scale
    )
    scores = jnp.where(allowed[None], scores, jnp.float32(-1000000000.0))
    row_max = jnp.max(scores, axis=-1, keepdims=True)
    weights = jnp.exp(scores - row_max)
    attn_probs = weights / jnp.sum(weights, axis=-1, keepdims=True)
    attn_probs = jnp.where(live_rows[None, :, None], attn_probs, jnp.float32(0.0))
    probs_b = attn_probs.astype(jnp.bfloat16)
    grad_v = jnp.einsum("hqk,qhd->kd", probs_b, o_group, preferred_element_type=jnp.float32)
    dprob = jnp.einsum("qhd,kd->hqk", o_group, v_group, preferred_element_type=jnp.float32)
    row_delta = jnp.sum(attn_probs * dprob, axis=-1, keepdims=True)
    dscore = (attn_probs * (dprob - row_delta) * score_scale).astype(jnp.bfloat16)
    grad_q = jnp.einsum("hqk,kd->qhd", dscore, k_group, preferred_element_type=jnp.float32)
    grad_k = jnp.einsum("hqk,qhd->kd", dscore, q_group, preferred_element_type=jnp.float32)
    return (
        grad_q.reshape(row_count, group_size * DH).astype(jnp.bfloat16),
        grad_k.astype(jnp.bfloat16),
        grad_v.astype(jnp.bfloat16),
    )


def local(hidden_in, queries, keys, values, grad_attn, send_rows, slot_docs):
    owners = lax.axis_size("dp")
    slot_count = send_rows.shape[0]
    tok_rows = queries.shape[0]
    live_send = send_rows >= 0
    pick_rows = jnp.maximum(send_rows, 0)
    grad_scale = 1.0 / math.sqrt(tok_rows * owners)

    def pack_rows(table):
        return jnp.where(live_send[:, :, None], table[pick_rows], jnp.zeros((), table.dtype))

    def flatten(block):
        return block.reshape(slot_count * owners, block.shape[2])

    def unflatten(block):
        return block.reshape(slot_count, owners, block.shape[1])

    targets = jnp.where(live_send, send_rows, tok_rows).reshape(-1)

    def place_rows(block):
        return (
            jnp.zeros((tok_rows, block.shape[2]), block.dtype)
            .at[targets]
            .set(flatten(block), mode="drop")
        )

    group_size = HQ // HK
    q_w, kv_w = group_size * DH, DH
    segment = jnp.broadcast_to(slot_docs[0][:, None], (slot_count, owners)).reshape(-1)
    dq_parts, dk_parts, dv_parts, wv_parts = [], [], [], []
    for head_kv in range(HK):
        q_cols = slice(head_kv * q_w, (head_kv + 1) * q_w)
        kv_cols = slice(head_kv * kv_w, (head_kv + 1) * kv_w)
        table = jnp.concatenate(
            (queries[:, q_cols], keys[:, kv_cols], values[:, kv_cols], grad_attn[:, q_cols]), axis=1
        )
        rows_in = flatten(
            lax.all_to_all(pack_rows(table), "dp", split_axis=1, concat_axis=1, tiled=True)
        )
        dq_rows, dk_rows, dv_rows = attend_group(
            rows_in[:, :q_w],
            rows_in[:, q_w : q_w + kv_w],
            rows_in[:, q_w + kv_w : q_w + 2 * kv_w],
            rows_in[:, q_w + 2 * kv_w :],
            segment,
        )
        rows_out = jnp.concatenate((dv_rows, dk_rows, dq_rows), axis=1)
        home = place_rows(
            lax.all_to_all(unflatten(rows_out), "dp", split_axis=1, concat_axis=1, tiled=True)
        )
        dv_home = home[:, :kv_w]
        dv_parts.append(dv_home)
        dk_parts.append(home[:, kv_w : 2 * kv_w])
        dq_parts.append(home[:, 2 * kv_w :])
        partial = jnp.einsum("td,tc->dc", hidden_in, dv_home, preferred_element_type=jnp.float32)
        partial = partial.reshape(owners, partial.shape[0] // owners, partial.shape[1])
        wv_parts.append(lax.all_to_all(partial, "dp", 0, 0, tiled=True).sum(0) * grad_scale)
    grad_queries = jnp.concatenate(dq_parts, axis=1)
    grad_keys = jnp.concatenate(dk_parts, axis=1)
    grad_values = jnp.concatenate(dv_parts, axis=1)
    grad_wv = jnp.concatenate(wv_parts, axis=1)
    return (grad_queries, grad_keys, grad_values, grad_wv)


def solution(mesh):
    placed = (
        P("dp", None),
        P("dp", None),
        P("dp", None),
        P("dp", None),
        P("dp", None),
        P(),
        P("dp", None),
    )
    return jax.shard_map(
        local,
        mesh=mesh,
        in_specs=placed,
        out_specs=(P("dp", None), P("dp", None), P("dp", None), P("dp", None)),
        check_vma=False,
    )
```

time: 452 us -> 473 us (1.046)
  the two profiles are of different devices: /device:TPU:103 before, /device:TPU:0 now
where the time goes in v1:
time: 473 us; the launch traced here: 464 us
  matrix products  123 us (26%)
  waiting for transfers between devices  118 us (25%)
  local copies, waits for them, and re-layouts  97.4 us (21%)
  starting transfers between devices  95.7 us (20%)
  other arithmetic  28.2 us (6%)
    all_to_all x4, waiting for transfers between devices, local(): lax.all_to_all(partial, 'dp', 0, 0, tiled=True).sum(0) * grad_scale  80.9 us
    all_to_all x4, starting transfers between devices, local(): lax.all_to_all(pack_rows(table), 'dp', split_axis=1, concat_axis=1, tiled...  36.3 us
    all_to_all x4, starting transfers between devices, local(): lax.all_to_all(unflatten(rows_out), 'dp', split_axis=1, concat_axis=1, ti...  35.9 us
    dot_general x4, matrix products, attend_group(): jnp.einsum('hqk,kd->qhd', dscore, k_group, preferred_element_type=jnp.flo...  34.9 us
    dot_general x4, matrix products, attend_group(): jnp.einsum('hqk,qhd->kd', dscore, q_group, preferred_element_type=jnp.flo...  33.4 us
    all_to_all x4, starting transfers between devices, local(): lax.all_to_all(partial, 'dp', 0, 0, tiled=True).sum(0) * grad_scale  23.5 us
    all_to_all x4, waiting for transfers between devices, local(): lax.all_to_all(pack_rows(table), 'dp', split_axis=1, concat_axis=1, tiled...  21.1 us
    sub x4, matrix products, attend_group(): weights = jnp.exp(scores - row_max)  18.9 us
  transfers between devices with their start and end apart: 12, of which 7 were waited for; matrix products, arithmetic and copies ran while one was open for 45% of the time, Pallas kernels for 0%

profile of v1, /device:TPU:0, one launch (start us, length us, event | category | flops | bytes accessed | tf_op | source)
XLA Modules:
  0.0 464.3 jit_solution(9664430870209603640)
XLA Ops:
  2.2 2.0 fusion.166
  4.2 2.0 fusion.167
  7.1 2.9 gather_fusion.2
  10.0 2.9 gather_fusion.3
  14.2 2.9 gather_fusion.1
  17.1 2.9 gather_fusion
  20.1 9.2 %copy_select_fusion.3 = (bf16[4,128,1280]{2,0,1:T(4,128)(2,1)}, bf16[4,128,1280]{2,0,1:T(4,128)(2,1)}, bf16[4,128,1280]{2,0,1:T(4,128)(2,1)}, bf16[4,128,1280]{2,0,1:T(4,128)(2,1)}) fusion(bf16[4,128,1280]{2,1,0:T(8,128)(2,1)} %bitcast.375, pred[4,128]{0,1:T(8,128)(4,1)S(1)} %copy.128, bf16[4,128,1280]{2,1,0:T(8,128)(2,1)} %bitcast.374, ...), kind=kLoop, calls=%fused_computation.91 | loop fusion | flops 2621440 | bytes 10486272 | tf_op jit(solution)/shard_map/jit(_where)/select_n | solution.py:58
  29.3 11.2 %all-to-all-start = ((bf16[4,128,1280]{2,0,1:T(4,128)(2,1)}), bf16[4,128,1280]{2,0,1:T(4,128)(2,1)S(1)}, u32[]{:S(2)}, u32[]{:S(2)}) async-start(bf16[4,128,1280]{2,0,1:T(4,128)(2,1)} %get-tuple-element.36), calls=%async_computation | async-start | bytes 2621440 | tf_op jit(solution)/shard_map/all_to_all | solution.py:86
  41.6 21.1 %all-to-all-done = bf16[4,128,1280]{2,0,1:T(4,128)(2,1)S(1)} async-done(((bf16[4,128,1280]{2,0,1:T(4,128)(2,1)}), bf16[4,128,1280]{2,0,1:T(4,128)(2,1)S(1)}, u32[]{:S(2)}, u32[]{:S(2)}) %all-to-all-start) | async-done | bytes 1310752 | tf_op jit(solution)/shard_map/all_to_all | solution.py:86
  63.7 4.8 %all-to-all-start.2 = ((bf16[4,128,1280]{2,0,1:T(4,128)(2,1)}), bf16[4,128,1280]{2,0,1:T(4,128)(2,1)S(1)}, u32[]{:S(2)}, u32[]{:S(2)}) async-start(bf16[4,128,1280]{2,0,1:T(4,128)(2,1)} %get-tuple-element.37), calls=%async_computation.2 | async-start | bytes 2621440 | tf_op jit(solution)/shard_map/all_to_all | solution.py:86
  72.2 2.0 copy.131
  74.2 4.7 %fusion.177 = (f32[4,512]{1,0:T(4,128)S(1)}, f32[4,512,512]{1,2,0:T(8,128)}) fusion(pred[512,512]{0,1:T(8,128)(4,1)} %fusion.93, bf16[512,4,128]{0,2,1:T(8,128)(2,1)} %bitcast.404, bf16[512,1280]{1,0:T(8,128)(2,1)} %bitcast.385), kind=kOutput, calls=%fused_computation.229 | convolution fusion | flops 272630272 | bytes 5120000 | tf_op jit(solution)/shard_map/sub | solution.py:32
  79.0 3.8 fusion.85
  83.8 3.8 fusion.104
  87.6 8.5 %fusion.88 = bf16[512,128]{0,1:T(8,128)(2,1)} fusion(bf16[512,4,128]{0,2,1:T(8,128)(2,1)} %bitcast.405, f32[512,512,4]{1,0,2:T(8,128)} %fusion.104, f32[4,512,512]{1,2,0:T(8,128)} %get-tuple-element.49, f32[4,512]{1,0:T(4,128)S(1)} %get-tuple-element.48, pred[512]{0:T(512)(128)(4,1)S(1)} %bitcast_compare_fusion), kind=kOutput, calls=%fused_computation.108 | convolution fusion | flops 277940736 | bytes 9052672 | tf_op jit(solution)/shard_map/hqk,qhd->kd/dot_general | solution.py:41
  97.7 8.7 %fusion.59 = bf16[128,4,512]{2,0,1:T(8,128)(2,1)} fusion(f32[512,512,4]{1,0,2:T(8,128)} %fusion.104, bf16[512,1280]{1,0:T(8,128)(2,1)} %bitcast.387, f32[4,512,512]{1,2,0:T(8,128)} %get-tuple-element.49, f32[4,512]{1,0:T(4,128)S(1)} %get-tuple-element.48, pred[512]{0:T(512)(128)(4,1)S(1)} %bitcast_compare_fusion), kind=kOutput, calls=%fused_computation.95 | convolution fusion | flops 278137344 | bytes 17449984 | tf_op jit(solution)/shard_map/hqk,kd->qhd/dot_general | solution.py:40
  106.4 2.0 copy.141
  109.5 10.3 %all-to-all-start.4 = ((bf16[4,128,1280]{2,0,1:T(4,128)(2,1)}), bf16[4,128,1280]{2,0,1:T(4,128)(2,1)S(1)}, u32[]{:S(2)}, u32[]{:S(2)}) async-start(bf16[4,128,1280]{2,0,1:T(4,128)(2,1)} %get-tuple-element.38), calls=%async_computation.4 | async-start | bytes 2621440 | tf_op jit(solution)/shard_map/all_to_all | solution.py:86
  123.4 2.1 copy.146
  125.5 4.7 %fusion.176 = (f32[4,512]{1,0:T(4,128)S(1)}, f32[4,512,512]{1,2,0:T(8,128)}) fusion(pred[512,512]{0,1:T(8,128)(4,1)} %fusion.93, bf16[512,4,128]{0,2,1:T(8,128)(2,1)} %bitcast.406, bf16[512,1280]{1,0:T(8,128)(2,1)} %bitcast.389), kind=kOutput, calls=%fused_computation.228 | convolution fusion | flops 272630272 | bytes 5120000 | tf_op jit(solution)/shard_map/sub | solution.py:32
  130.2 3.8 fusion.82
  135.6 3.8 fusion.101
  139.4 8.5 %fusion.89 = bf16[512,128]{0,1:T(8,128)(2,1)} fusion(bf16[512,4,128]{0,2,1:T(8,128)(2,1)} %bitcast.407, f32[512,512,4]{1,0,2:T(8,128)} %fusion.101, f32[4,512,512]{1,2,0:T(8,128)} %get-tuple-element.47, f32[4,512]{1,0:T(4,128)S(1)} %get-tuple-element.46, pred[512]{0:T(512)(128)(4,1)S(1)} %bitcast_compare_fusion), kind=kOutput, calls=%fused_computation.109 | convolution fusion | flops 277940736 | bytes 9052672 | tf_op jit(solution)/shard_map/hqk,qhd->kd/dot_general | solution.py:41
  149.6 8.7 %fusion.58 = bf16[128,4,512]{2,0,1:T(8,128)(2,1)} fusion(f32[512,512,4]{1,0,2:T(8,128)} %fusion.101, bf16[512,1280]{1,0:T(8,128)(2,1)} %bitcast.391, f32[4,512,512]{1,2,0:T(8,128)} %get-tuple-element.47, f32[4,512]{1,0:T(4,128)S(1)} %get-tuple-element.46, pred[512]{0:T(512)(128)(4,1)S(1)} %bitcast_compare_fusion), kind=kOutput, calls=%fused_computation.94 | convolution fusion | flops 278137344 | bytes 17449984 | tf_op jit(solution)/shard_map/hqk,kd->qhd/dot_general | solution.py:40
  158.3 2.1 copy.156
  161.5 10.0 %all-to-all-start.6 = ((bf16[4,128,1280]{2,0,1:T(4,128)(2,1)}), bf16[4,128,1280]{2,0,1:T(4,128)(2,1)S(1)}, u32[]{:S(2)}, u32[]{:S(2)}) async-start(bf16[4,128,1280]{2,0,1:T(4,128)(2,1)} %get-tuple-element.39), calls=%async_computation.6 | async-start | bytes 2621440 | tf_op jit(solution)/shard_map/all_to_all | solution.py:86
  175.1 2.1 copy.161
  177.2 4.7 %fusion.175 = (f32[4,512]{1,0:T(4,128)S(1)}, f32[4,512,512]{1,2,0:T(8,128)}) fusion(pred[512,512]{0,1:T(8,128)(4,1)} %fusion.93, bf16[512,4,128]{0,2,1:T(8,128)(2,1)} %bitcast.402, bf16[512,1280]{1,0:T(8,128)(2,1)} %bitcast.381), kind=kOutput, calls=%fused_computation.227 | convolution fusion | flops 272630272 | bytes 5120000 | tf_op jit(solution)/shard_map/sub | solution.py:32
  190.2 3.8 fusion.98
  194.0 8.5 %fusion.90 = bf16[512,128]{0,1:T(8,128)(2,1)} fusion(bf16[512,4,128]{0,2,1:T(8,128)(2,1)} %bitcast.403, f32[512,512,4]{1,0,2:T(8,128)} %fusion.98, f32[4,512,512]{1,2,0:T(8,128)} %get-tuple-element.45, f32[4,512]{1,0:T(4,128)S(1)} %get-tuple-element.44, pred[512]{0:T(512)(128)(4,1)S(1)} %bitcast_compare_fusion), kind=kOutput, calls=%fused_computation.110 | convolution fusion | flops 277940736 | bytes 9052672 | tf_op jit(solution)/shard_map/hqk,qhd->kd/dot_general | solution.py:41
  204.2 10.3 %all-to-all-start.1 = ((bf16[4,128,768]{2,0,1:T(4,128)(2,1)}), bf16[4,128,768]{2,0,1:T(4,128)(2,1)}, u32[]{:S(2)}, u32[]{:S(2)}) async-start(bf16[4,128,768]{2,0,1:T(4,128)(2,1)} %copy.142), calls=%async_computation.1 | async-start | bytes 1572864 | tf_op jit(solution)/shard_map/all_to_all | solution.py:97
  214.5 8.8 %fusion.57 = bf16[128,4,512]{2,0,1:T(8,128)(2,1)} fusion(f32[512,512,4]{1,0,2:T(8,128)} %fusion.98, bf16[512,1280]{1,0:T(8,128)(2,1)} %bitcast.383, f32[4,512,512]{1,2,0:T(8,128)} %get-tuple-element.45, f32[4,512]{1,0:T(4,128)S(1)} %get-tuple-element.44, pred[512]{0:T(512)(128)(4,1)S(1)} %bitcast_compare_fusion), kind=kOutput, calls=%fused_computation.93 | convolution fusion | flops 278137344 | bytes 17449984 | tf_op jit(solution)/shard_map/hqk,kd->qhd/dot_general | solution.py:40
  223.3 2.1 copy.171
  228.6 4.8 %fusion.174 = (f32[4,512]{1,0:T(4,128)S(1)}, f32[4,512,512]{1,2,0:T(8,128)}) fusion(pred[512,512]{0,1:T(8,128)(4,1)} %fusion.93, bf16[512,4,128]{0,2,1:T(8,128)(2,1)} %bitcast.400, bf16[512,1280]{1,0:T(8,128)(2,1)} %bitcast.377), kind=kOutput, calls=%fused_computation.226 | convolution fusion | flops 272630272 | bytes 5120000 | tf_op jit(solution)/shard_map/sub | solution.py:32
  233.3 9.7 %all-to-all-start.3 = ((bf16[4,128,768]{2,0,1:T(4,128)(2,1)}), bf16[4,128,768]{2,0,1:T(4,128)(2,1)S(1)}, u32[]{:S(2)}, u32[]{:S(2)}) async-start(bf16[4,128,768]{2,0,1:T(4,128)(2,1)} %copy.157), calls=%async_computation.3 | async-start | bytes 1572864 | tf_op jit(solution)/shard_map/all_to_all | solution.py:97
  245.5 3.9 fusion.76
  249.4 10.2 %all-to-all-done.3 = bf16[4,128,768]{2,0,1:T(4,128)(2,1)S(1)} async-done(((bf16[4,128,768]{2,0,1:T(4,128)(2,1)}), bf16[4,128,768]{2,0,1:T(4,128)(2,1)S(1)}, u32[]{:S(2)}, u32[]{:S(2)}) %all-to-all-start.3) | async-done | bytes 786464 | tf_op jit(solution)/shard_map/all_to_all | solution.py:97
  259.6 5.7 %all-to-all-start.5 = ((bf16[4,128,768]{2,0,1:T(4,128)(2,1)}), bf16[4,128,768]{2,0,1:T(4,128)(2,1)}, u32[]{:S(2)}, u32[]{:S(2)}) async-start(bf16[4,128,768]{2,0,1:T(4,128)(2,1)} %copy.172), calls=%async_computation.5 | async-start | bytes 1572864 | tf_op jit(solution)/shard_map/all_to_all | solution.py:97
  265.3 3.6 fusion.95
  269.9 7.9 %fusion.91 = bf16[512,128]{0,1:T(8,128)(2,1)S(1)} fusion(bf16[512,4,128]{0,2,1:T(8,128)(2,1)} %bitcast.401, f32[512,512,4]{1,0,2:T(8,128)} %fusion.95, f32[4,512,512]{1,2,0:T(8,128)} %get-tuple-element.43, f32[4,512]{1,0:T(4,128)S(1)} %get-tuple-element.42, pred[512]{0:T(512)(128)(4,1)S(1)} %bitcast_compare_fusion), kind=kOutput, calls=%fused_computation.111 | convolution fusion | flops 277940736 | bytes 9052672 | tf_op jit(solution)/shard_map/hqk,qhd->kd/dot_general | solution.py:41
  278.5 8.7 %fusion.56 = bf16[128,4,512]{2,0,1:T(8,128)(2,1)} fusion(f32[512,512,4]{1,0,2:T(8,128)} %fusion.95, bf16[512,1280]{1,0:T(8,128)(2,1)} %bitcast.379, f32[4,512,512]{1,2,0:T(8,128)} %get-tuple-element.43, f32[4,512]{1,0:T(4,128)S(1)} %get-tuple-element.42, pred[512]{0:T(512)(128)(4,1)S(1)} %bitcast_compare_fusion), kind=kOutput, calls=%fused_computation.92 | convolution fusion | flops 278137344 | bytes 17449984 | tf_op jit(solution)/shard_map/hqk,kd->qhd/dot_general | solution.py:40
  291.0 10.2 %all-to-all-start.7 = ((bf16[4,128,768]{2,0,1:T(4,128)(2,1)}), bf16[4,128,768]{2,0,1:T(4,128)(2,1)}, u32[]{:S(2)}, u32[]{:S(2)}) async-start(bf16[4,128,768]{2,0,1:T(4,128)(2,1)} %copy.187), calls=%async_computation.7 | async-start | bytes 1572864 | tf_op jit(solution)/shard_map/all_to_all | solution.py:97
  301.1 2.1 copy.143
  303.2 3.3 scatter_custom_fusion
  308.4 2.9 copy.189
  311.2 6.1 %all-to-all-done.7 = bf16[4,128,768]{2,0,1:T(4,128)(2,1)} async-done(((bf16[4,128,768]{2,0,1:T(4,128)(2,1)}), bf16[4,128,768]{2,0,1:T(4,128)(2,1)}, u32[]{:S(2)}, u32[]{:S(2)}) %all-to-all-start.7) | async-done | bytes 786464 | tf_op jit(solution)/shard_map/all_to_all | solution.py:97
  317.3 6.0 %all-to-all-start.8 = ((f32[128,32,128]{2,1,0:T(8,128)}), f32[128,32,128]{2,1,0:T(8,128)}, u32[]{:S(2)}, u32[]{:S(2)}) async-start(f32[128,32,128]{2,1,0:T(8,128)} %bitcast.370), calls=%async_computation.8 | async-start | bytes 4194304 | tf_op jit(solution)/shard_map/all_to_all | solution.py:105
  324.3 3.3 scatter_custom_fusion.1
  329.4 2.9 copy.190
  332.3 21.2 %all-to-all-done.8 = f32[128,32,128]{2,1,0:T(8,128)} async-done(((f32[128,32,128]{2,1,0:T(8,128)}), f32[128,32,128]{2,1,0:T(8,128)}, u32[]{:S(2)}, u32[]{:S(2)}) %all-to-all-start.8) | async-done | bytes 2097184 | tf_op jit(solution)/shard_map/all_to_all | solution.py:105
  353.5 5.8 %all-to-all-start.9 = ((f32[128,32,128]{2,1,0:T(8,128)}), f32[128,32,128]{2,1,0:T(8,128)}, u32[]{:S(2)}, u32[]{:S(2)}) async-start(f32[128,32,128]{2,1,0:T(8,128)} %bitcast.371), calls=%async_computation.9 | async-start | bytes 4194304 | tf_op jit(solution)/shard_map/all_to_all | solution.py:105
  359.3 2.1 copy.173
  361.4 3.3 scatter_custom_fusion.2
  364.7 1.9 convolution_bitcast_fusion.1
  366.5 2.9 copy.191
  369.4 20.0 %all-to-all-done.9 = f32[128,32,128]{2,1,0:T(8,128)} async-done(((f32[128,32,128]{2,1,0:T(8,128)}), f32[128,32,128]{2,1,0:T(8,128)}, u32[]{:S(2)}, u32[]{:S(2)}) %all-to-all-start.9) | async-done | bytes 2097184 | tf_op jit(solution)/shard_map/all_to_all | solution.py:105
  389.5 5.8 %all-to-all-start.10 = ((f32[128,32,128]{2,1,0:T(8,128)}), f32[128,32,128]{2,1,0:T(8,128)}, u32[]{:S(2)}, u32[]{:S(2)}) async-start(f32[128,32,128]{2,1,0:T(8,128)} %bitcast.369), calls=%async_computation.10 | async-start | bytes 4194304 | tf_op jit(solution)/shard_map/all_to_all | solution.py:105
  395.2 2.1 copy.188
  397.3 3.9 scatter_custom_fusion.3
  401.3 2.6 convolution_bitcast_fusion
  403.9 3.0 copy.192
  406.8 18.6 %all-to-all-done.10 = f32[128,32,128]{2,1,0:T(8,128)} async-done(((f32[128,32,128]{2,1,0:T(8,128)}), f32[128,32,128]{2,1,0:T(8,128)}, u32[]{:S(2)}, u32[]{:S(2)}) %all-to-all-start.10) | async-done | bytes 2097184 | tf_op jit(solution)/shard_map/all_to_all | solution.py:105
  425.4 5.9 %all-to-all-start.11 = ((f32[128,32,128]{2,1,0:T(8,128)}), f32[128,32,128]{2,1,0:T(8,128)}, u32[]{:S(2)}, u32[]{:S(2)}) async-start(f32[128,32,128]{2,1,0:T(8,128)} %bitcast.368), calls=%async_computation.11 | async-start | bytes 4194304 | tf_op jit(solution)/shard_map/all_to_all | solution.py:105
  440.3 21.2 %all-to-all-done.11 = f32[128,32,128]{2,1,0:T(8,128)} async-done(((f32[128,32,128]{2,1,0:T(8,128)}), f32[128,32,128]{2,1,0:T(8,128)}, u32[]{:S(2)}, u32[]{:S(2)}) %all-to-all-start.11) | async-done | bytes 2097184 | tf_op jit(solution)/shard_map/all_to_all | solution.py:105
  (98 shorter events, 62.0 us)
Async XLA Ops:
  0.6 305.9 %copy-start = (bf16[256,4096]{1,0:T(8,128)(2,1)S(1)}, bf16[256,4096]{1,0:T(8,128)(2,1)}, u32[]{:S(2)}) copy-start(bf16[256,4096]{1,0:T(8,128)(2,1)} %param.7) | copy-start | bytes 6291460
  0.6 5.6 %copy-start.11 = (bf16[256,512]{1,0:T(8,128)(2,1)S(1)}, bf16[256,512]{1,0:T(8,128)(2,1)}, u32[]{:S(2)}) copy-start(bf16[256,512]{1,0:T(8,128)(2,1)} %param.9) | copy-start | bytes 786436
  0.7 5.7 %copy-start.12 = (bf16[256,512]{1,0:T(8,128)(2,1)S(1)}, bf16[256,512]{1,0:T(8,128)(2,1)}, u32[]{:S(2)}) copy-start(bf16[256,512]{1,0:T(8,128)(2,1)} %param.10) | copy-start | bytes 786436
  20.1 20.4 %copy-start.13 = (s32[1,4]{1,0:T(1,128)S(1)}, s32[1,4]{1,0:T(1,128)}, u32[]{:S(2)}) copy-start(s32[1,4]{1,0:T(1,128)} %param.13) | copy-start | bytes 52
  29.3 33.3 %all-to-all-start = ((bf16[4,128,1280]{2,0,1:T(4,128)(2,1)}), bf16[4,128,1280]{2,0,1:T(4,128)(2,1)S(1)}, u32[]{:S(2)}, u32[]{:S(2)}) async-start(bf16[4,128,1280]{2,0,1:T(4,128)(2,1)} %get-tuple-element.36), calls=%async_computation | async-start | bytes 2621440 | tf_op jit(solution)/shard_map/all_to_all | solution.py:86
  62.6 1.1 copy-start.3
  63.7 44.8 %all-to-all-start.2 = ((bf16[4,128,1280]{2,0,1:T(4,128)(2,1)}), bf16[4,128,1280]{2,0,1:T(4,128)(2,1)S(1)}, u32[]{:S(2)}, u32[]{:S(2)}) async-start(bf16[4,128,1280]{2,0,1:T(4,128)(2,1)} %get-tuple-element.37), calls=%async_computation.2 | async-start | bytes 2621440 | tf_op jit(solution)/shard_map/all_to_all | solution.py:86
  70.0 1.1 copy-start.6
  108.5 1.1 copy-start.2
  109.5 50.8 %all-to-all-start.4 = ((bf16[4,128,1280]{2,0,1:T(4,128)(2,1)}), bf16[4,128,1280]{2,0,1:T(4,128)(2,1)S(1)}, u32[]{:S(2)}, u32[]{:S(2)}) async-start(bf16[4,128,1280]{2,0,1:T(4,128)(2,1)} %get-tuple-element.38), calls=%async_computation.4 | async-start | bytes 2621440 | tf_op jit(solution)/shard_map/all_to_all | solution.py:86
  121.3 1.1 copy-start.7
  160.4 1.1 copy-start.1
  161.5 42.7 %all-to-all-start.6 = ((bf16[4,128,1280]{2,0,1:T(4,128)(2,1)}), bf16[4,128,1280]{2,0,1:T(4,128)(2,1)S(1)}, u32[]{:S(2)}, u32[]{:S(2)}) async-start(bf16[4,128,1280]{2,0,1:T(4,128)(2,1)} %get-tuple-element.39), calls=%async_computation.6 | async-start | bytes 2621440 | tf_op jit(solution)/shard_map/all_to_all | solution.py:86
  173.0 1.1 copy-start.5
  181.9 5.8 %copy-start.10 = (bf16[64,4,8,128]{3,2,1,0:T(8,128)(2,1)S(1)}, bf16[64,4,8,128]{3,2,1,0:T(8,128)(2,1)}, u32[]{:S(2)}) copy-start(bf16[64,4,8,128]{3,2,1,0:T(8,128)(2,1)} %get-tuple-element.9) | copy-start | bytes 1572868
  181.9 5.8 %copy-start.14 = (f32[4,512,512]{1,2,0:T(8,128)S(1)}, f32[4,512,512]{1,2,0:T(8,128)}, u32[]{:S(2)}) copy-start(f32[4,512,512]{1,2,0:T(8,128)} %get-tuple-element.45) | copy-start | bytes 12582916
  204.2 29.1 %all-to-all-start.1 = ((bf16[4,128,768]{2,0,1:T(4,128)(2,1)}), bf16[4,128,768]{2,0,1:T(4,128)(2,1)}, u32[]{:S(2)}, u32[]{:S(2)}) async-start(bf16[4,128,768]{2,0,1:T(4,128)(2,1)} %copy.142), calls=%async_computation.1 | async-start | bytes 1572864 | tf_op jit(solution)/shard_map/all_to_all | solution.py:97
  225.5 1.2 copy-start.4
  228.6 14.5 %copy-start.8 = (bf16[512,512]{1,0:T(8,128)(2,1)S(1)}, bf16[512,512]{1,0:T(8,128)(2,1)}, u32[]{:S(2)}) copy-start(bf16[512,512]{1,0:T(8,128)(2,1)} %copy.171) | copy-start | bytes 1572868
  233.3 26.2 %all-to-all-start.3 = ((bf16[4,128,768]{2,0,1:T(4,128)(2,1)}), bf16[4,128,768]{2,0,1:T(4,128)(2,1)S(1)}, u32[]{:S(2)}, u32[]{:S(2)}) async-start(bf16[4,128,768]{2,0,1:T(4,128)(2,1)} %copy.157), calls=%async_computation.3 | async-start | bytes 1572864 | tf_op jit(solution)/shard_map/all_to_all | solution.py:97
  245.5 19.8 %copy-start.9 = (bf16[64,4,8,128]{3,2,1,0:T(8,128)(2,1)S(1)}, bf16[64,4,8,128]{3,2,1,0:T(8,128)(2,1)}, u32[]{:S(2)}) copy-start(bf16[64,4,8,128]{3,2,1,0:T(8,128)(2,1)} %get-tuple-element.11) | copy-start | bytes 1572868
  259.6 31.4 %all-to-all-start.5 = ((bf16[4,128,768]{2,0,1:T(4,128)(2,1)}), bf16[4,128,768]{2,0,1:T(4,128)(2,1)}, u32[]{:S(2)}, u32[]{:S(2)}) async-start(bf16[4,128,768]{2,0,1:T(4,128)(2,1)} %copy.172), calls=%async_computation.5 | async-start | bytes 1572864 | tf_op jit(solution)/shard_map/all_to_all | solution.py:97
  291.0 26.4 %all-to-all-start.7 = ((bf16[4,128,768]{2,0,1:T(4,128)(2,1)}), bf16[4,128,768]{2,0,1:T(4,128)(2,1)}, u32[]{:S(2)}, u32[]{:S(2)}) async-start(bf16[4,128,768]{2,0,1:T(4,128)(2,1)} %copy.187), calls=%async_computation.7 | async-start | bytes 1572864 | tf_op jit(solution)/shard_map/all_to_all | solution.py:97
  317.3 36.2 %all-to-all-start.8 = ((f32[128,32,128]{2,1,0:T(8,128)}), f32[128,32,128]{2,1,0:T(8,128)}, u32[]{:S(2)}, u32[]{:S(2)}) async-start(f32[128,32,128]{2,1,0:T(8,128)} %bitcast.370), calls=%async_computation.8 | async-start | bytes 4194304 | tf_op jit(solution)/shard_map/all_to_all | solution.py:105
  353.5 35.9 %all-to-all-start.9 = ((f32[128,32,128]{2,1,0:T(8,128)}), f32[128,32,128]{2,1,0:T(8,128)}, u32[]{:S(2)}, u32[]{:S(2)}) async-start(f32[128,32,128]{2,1,0:T(8,128)} %bitcast.371), calls=%async_computation.9 | async-start | bytes 4194304 | tf_op jit(solution)/shard_map/all_to_all | solution.py:105
  389.5 35.9 %all-to-all-start.10 = ((f32[128,32,128]{2,1,0:T(8,128)}), f32[128,32,128]{2,1,0:T(8,128)}, u32[]{:S(2)}, u32[]{:S(2)}) async-start(f32[128,32,128]{2,1,0:T(8,128)} %bitcast.369), calls=%async_computation.10 | async-start | bytes 4194304 | tf_op jit(solution)/shard_map/all_to_all | solution.py:105
  425.4 8.4 %slice-start = ((bf16[256,768]{1,0:T(8,128)(2,1)}), bf16[256,512]{1,0:T(8,128)(2,1)S(1)}, s32[]{:S(2)}) async-start(bf16[256,768]{1,0:T(8,128)(2,1)} %scatter_custom_fusion.3), calls=%async_computation.12 | async-start | bytes 524288 | tf_op jit(solution)/shard_map/slice | solution.py:102
  425.4 36.1 %all-to-all-start.11 = ((f32[128,32,128]{2,1,0:T(8,128)}), f32[128,32,128]{2,1,0:T(8,128)}, u32[]{:S(2)}, u32[]{:S(2)}) async-start(f32[128,32,128]{2,1,0:T(8,128)} %bitcast.368), calls=%async_computation.11 | async-start | bytes 4194304 | tf_op jit(solution)/shard_map/all_to_all | solution.py:105
